TPU v7x, 512 devices: a whole 4x8x8 slice. The times are simulated.
512 devices in a mesh: row: 8 (over x, y_lo), col: 8 (over y_hi, core), smp: 8 (over z).
Axes of the slice: x: 4, y: 8 (y_hi: 4, y_lo: 2; y = y_hi * 2 + y_lo), z: 8, core: 2. Of those that a mesh axis runs over, the one named last changes fastest.
Arguments:
- single: bfloat16 [1024, 768], P('row'), may hold values from -0.59765625 to 0.59765625
- pair_features: bfloat16 [1024, 1024, 128], P('row', ('col', 'smp')), may hold values from -6 to 6
- coords: float32 [3, 8192], replicated, may hold values from -6 to 6
- token_centre_atom: int32 [1024], P('row'), may hold values from 0 to 8191
- chain_label: int32 [1024], P('row'), may hold values from 0 to 7, never falling along the last dimension, each value on 1 to 256 neighbouring positions
- padding_key_mask: int32 [1024], P('row'), may hold values 0 or 1
- angles: float32 [8, 3], P('smp'), may hold values from -3.140625 to 3.140625
- sample_noise_level: float32 [8], P('smp'), may hold values from 0.05 to 10
- centre_noise: float32 [8, 3, 1024], P('smp', None, 'row'), may hold values from -6 to 6
- embedding_weight: float32 [4, 768], replicated, may hold values from -1.5 to 1.5
- pair_bias_weight: bfloat16 [128, 4, 16], replicated, may hold values from -1 to 1
- same_chain_offset: float32 [4, 16], replicated, may hold values from -300 to 300
- query_key_value_gate_weight: bfloat16 [4, 4, 768, 768], P(None, None, 'col'), may hold values from -0.21875 to 0.21875
- attention_output_weight: bfloat16 [4, 768, 768], P(None, 'col'), may hold values from -1.25 to 1.25
- position_update_weight: bfloat16 [3, 768], replicated, may hold values from -0.21875 to 0.21875
Outputs:
- tokens_out: bfloat16 [8, 1024, 768], P('smp', 'row')
- denoised: float32 [8, 3, 1024], P('smp', None, 'row')
All inputs are finite; a program needn't handle non-finite values. No bound on the sum of `padding_key_mask` on one device may be relied on, other than what follows from the above.
Results may differ from a plain program's by a relative error of at most 0.024.
Values may be sent and summed in bfloat16 or wider, within the bound.
No kernel may reach another device: no remote copies, remote signals or barrier semaphores. Data moves between devices by JAX's collectives and lax.ppermute only.
A program may use at most 64 MiB of HBM per device.

v0:
```python
import jax
import jax.numpy as jnp
from jax import lax
from jax.sharding import PartitionSpec as P

EPSILON = 1e-05
MASKED = -1000000000.0
LOWEST = -1e30


def layer_norm(inputs):
    average = jnp.mean(inputs, axis=-1, keepdims=True)
    centred = inputs - average
    spread = jnp.mean(centred * centred, axis=-1, keepdims=True)
    return centred * lax.rsqrt(spread + EPSILON)


def rotation_rows(angles):
    cos_a = jnp.cos(angles[:, 0])
    sin_a = jnp.sin(angles[:, 0])
    cos_b = jnp.cos(angles[:, 1])
    sin_b = jnp.sin(angles[:, 1])
    cos_c = jnp.cos(angles[:, 2])
    sin_c = jnp.sin(angles[:, 2])
    first = jnp.stack(
        [
            cos_a * cos_b,
            cos_a * sin_b * sin_c - sin_a * cos_c,
            cos_a * sin_b * cos_c + sin_a * sin_c,
        ],
        axis=-1,
    )
    second = jnp.stack(
        [
            sin_a * cos_b,
            sin_a * sin_b * sin_c + cos_a * cos_c,
            sin_a * sin_b * cos_c - cos_a * sin_c,
        ],
        axis=-1,
    )
    third = jnp.stack([-sin_b, cos_b * sin_c, cos_b * cos_c], axis=-1)
    return jnp.stack([first, second, third], axis=1)


def noisy_centres(coords, token_centre_atom, angles, sample_noise_level, centre_noise):
    centre = jnp.take(coords, token_centre_atom, axis=1)
    rotation = rotation_rows(angles)
    turned = rotation[:, :, 0, None] * centre[0][None, None, :]
    turned = turned + rotation[:, :, 1, None] * centre[1][None, None, :]
    turned = turned + rotation[:, :, 2, None] * centre[2][None, None, :]
    return turned + sample_noise_level[:, None, None] * centre_noise


def embed_tokens(single, noisy, sample_noise_level, embedding_weight):
    scaled = noisy / jnp.sqrt(sample_noise_level * sample_noise_level + 1.0)[:, None, None]
    log_level = 0.25 * jnp.log(sample_noise_level)
    hidden_activity = single.astype(jnp.float32)[None] + scaled[:, 0, :, None] * embedding_weight[0]
    hidden_activity = hidden_activity + scaled[:, 1, :, None] * embedding_weight[1]
    hidden_activity = hidden_activity + scaled[:, 2, :, None] * embedding_weight[2]
    hidden_activity = hidden_activity + log_level[:, None, None] * embedding_weight[3]
    return hidden_activity.astype(jnp.bfloat16)


def relay_bias(local_bias):
    blocks, total_heads, row_count, keys_dev = local_bias.shape
    col_count = lax.axis_size("col")
    copies = lax.axis_size("smp")
    group_members = total_heads // col_count
    spread = jnp.broadcast_to(
        local_bias.reshape(blocks, col_count, 1, group_members, row_count, 1, keys_dev),
        (blocks, col_count, copies, group_members, row_count, 1, keys_dev),
    )
    spread = spread.reshape(blocks, col_count * copies * group_members, row_count, 1, keys_dev)
    relayed = lax.all_to_all(spread, ("col", "smp"), split_axis=1, concat_axis=3, tiled=True)
    return relayed.reshape(blocks, group_members, row_count, -1)


def build_absorber(
    query_vectors,
    per_block_bias,
    chain_offset,
    query_chain_labels,
    gathered_chain_ids,
    gathered_key_mask,
    input_scaling,
):
    samples, row_count, group_members, head_size = query_vectors.shape

    def absorb(running, kv_piece, key_start):
        key_count = kv_piece.shape[0]
        key_rows = kv_piece[:, :, 0].reshape(key_count, samples, group_members, head_size)
        value_rows = kv_piece[:, :, 1].reshape(key_count, samples, group_members, head_size)
        attention_logits = (
            jnp.einsum(
                "sqhd,kshd->shqk", query_vectors, key_rows, preferred_element_type=jnp.float32
            )
            * input_scaling
        )
        bias_section = per_block_bias.astype(jnp.float32)
        chain_match = (query_chain_labels[:, None] == gathered_chain_ids[None, :]).astype(
            jnp.float32
        )
        attention_logits = (
            attention_logits
            + bias_section[None]
            + chain_offset[None, :, None, None] * chain_match[None, None]
        )
        attention_logits = jnp.where(
            gathered_key_mask[None, None, None, :] > 0, attention_logits, MASKED
        )
        old_max, old_sum, old_acc = running
        new_max = jnp.maximum(old_max, jnp.max(attention_logits, axis=-1))
        unscaled = jnp.exp(attention_logits - new_max[..., None])
        new_sum = jnp.sum(unscaled, axis=-1)
        new_acc = jnp.einsum(
            "shqk,kshd->shqd",
            unscaled.astype(jnp.bfloat16),
            value_rows,
            preferred_element_type=jnp.float32,
        )
        return (new_max, new_sum, new_acc)

    return absorb


def body(
    single,
    pair_features,
    coords,
    token_centre_atom,
    chain_label,
    padding_key_mask,
    angles,
    sample_noise_level,
    centre_noise,
    embedding_weight,
    pair_bias_weight,
    same_chain_offset,
    query_key_value_gate_weight,
    attention_output_weight,
    position_update_weight,
):
    noisy = noisy_centres(coords, token_centre_atom, angles, sample_noise_level, centre_noise)
    hidden_activity = embed_tokens(single, noisy, sample_noise_level, embedding_weight)
    pair_normed = layer_norm(pair_features.astype(jnp.float32)).astype(jnp.bfloat16)
    local_bias = jnp.einsum(
        "ikc,cbh->bhik", pair_normed, pair_bias_weight, preferred_element_type=jnp.float32
    ).astype(jnp.bfloat16)
    gathered_pair_bias = relay_bias(local_bias)
    gathered_chain_ids, gathered_key_mask = (
        lax.all_gather(chain_label, "row", axis=0, tiled=True),
        lax.all_gather(padding_key_mask, "row", axis=0, tiled=True),
    )
    samples, row_count, model_width = hidden_activity.shape
    group_members = gathered_pair_bias.shape[1]
    head_size = query_key_value_gate_weight.shape[2] // group_members
    group_offset = lax.axis_index("col") * group_members
    input_scaling = head_size ** (-0.5)
    for block_index in range(query_key_value_gate_weight.shape[0]):
        normed = layer_norm(hidden_activity.astype(jnp.float32)).astype(jnp.bfloat16)
        front = jnp.einsum(
            "snd,fed->fsne",
            normed,
            query_key_value_gate_weight[block_index, 0:2],
            preferred_element_type=jnp.float32,
        )
        key_value = jnp.einsum(
            "snd,fed->nsfe",
            normed,
            query_key_value_gate_weight[block_index, 2:4],
            preferred_element_type=jnp.float32,
        ).astype(jnp.bfloat16)
        query_vectors = (
            front[0].astype(jnp.bfloat16).reshape(samples, row_count, group_members, head_size)
        )
        chain_offset = lax.dynamic_slice_in_dim(
            same_chain_offset[block_index], group_offset, group_members, 0
        )
        absorb = build_absorber(
            query_vectors,
            gathered_pair_bias[block_index],
            chain_offset,
            chain_label,
            gathered_chain_ids,
            gathered_key_mask,
            input_scaling,
        )
        start_state = (
            jnp.full((samples, group_members, row_count), LOWEST, jnp.float32),
            jnp.zeros((samples, group_members, row_count), jnp.float32),
            jnp.zeros((samples, group_members, row_count, head_size), jnp.float32),
        )
        final_max, final_sum, final_acc = absorb(
            start_state, lax.all_gather(key_value, "row", axis=0, tiled=True), jnp.int32(0)
        )
        attended = final_acc / final_sum[..., None]
        attended = jnp.transpose(attended, (0, 2, 1, 3)).reshape(
            samples, row_count, group_members * head_size
        )
        gated_output = (jax.nn.sigmoid(front[1]) * attended).astype(jnp.bfloat16)
        partial_out = jnp.einsum(
            "kxp,pj->kxj",
            gated_output,
            attention_output_weight[block_index],
            preferred_element_type=jnp.float32,
        )
        summed = lax.psum(partial_out.astype(jnp.bfloat16), "col").astype(jnp.float32)
        hidden_activity = (hidden_activity.astype(jnp.float32) + summed).astype(jnp.bfloat16)
    final_normed = layer_norm(hidden_activity.astype(jnp.float32)).astype(jnp.bfloat16)
    update = jnp.einsum(
        "snd,cd->scn", final_normed, position_update_weight, preferred_element_type=jnp.float32
    )
    spread_sq = 1.0 + sample_noise_level * sample_noise_level
    denoised = (
        noisy / spread_sq[:, None, None]
        + (sample_noise_level / jnp.sqrt(spread_sq))[:, None, None] * update
    )
    return (hidden_activity, denoised)


def solution(mesh):
    return jax.shard_map(
        body,
        mesh=mesh,
        in_specs=(
            P("row", None),
            P("row", ("col", "smp"), None),
            P(),
            P("row"),
            P("row"),
            P("row"),
            P("smp", None),
            P("smp"),
            P("smp", None, "row"),
            P(),
            P(),
            P(),
            P(None, None, "col", None),
            P(None, "col", None),
            P(),
        ),
        out_specs=(P("smp", "row", None), P("smp", None, "row")),
        check_vma=False,
    )
```

profile of v0, /device:TPU:17, one launch (start us, length us, event | category | flops | bytes accessed | tf_op | source)
XLA Modules:
  0.0 548.1 jit_solution(17188569693350493762)
XLA Ops:
  7.2 1.4 convert_reduce_fusion
  8.6 1.7 fusion.36
  10.3 1.6 fusion.50
  12.4 1.9 broadcast_in_dim.47
  14.3 16.9 %all-to-all-start = ((bf16[4,128,128,1,16]{2,4,3,0,1:T(8,128)(2,1)}), bf16[4,128,128,1,16]{2,4,3,0,1:T(8,128)(2,1)S(1)}, u32[]{:S(2)}, u32[]{:S(2)}) async-start(bf16[4,128,128,1,16]{2,4,3,0,1:T(8,128)(2,1)} %bitcast.262), calls=%async_computation | async-start | bytes 4194304 | tf_op jit(solution)/shard_map/all_to_all | solution.py:74
  36.9 2.6 copy.35
  39.5 2.8 gather_fusion
  45.0 41.1 %all-gather.1 = s32[8,1,128]{2,1,0:T(1,128)S(1)} all-gather(s32[1,1,128]{2,1,0:T(1,128)S(1)} %bitcast.290), channel_id=1, replica_groups=mesh['row'=8,'col'=8,'smp'=8] {'row'}, dimensions={0}, use_global_device_ids=true | all-gather | bytes 4608 | tf_op jit(solution)/shard_map/all_gather | solution.py:151
  86.1 11.5 %all-gather = s32[8,1,128]{2,1,0:T(1,128)S(1)} all-gather(s32[1,1,128]{2,1,0:T(1,128)S(1)} %bitcast.291), channel_id=1, replica_groups=mesh['row'=8,'col'=8,'smp'=8] {'row'}, dimensions={0}, use_global_device_ids=true | all-gather | bytes 4608 | tf_op jit(solution)/shard_map/all_gather | solution.py:152
  99.0 21.4 %all_gather.19 = bf16[1024,1,2,96]{0,3,2,1:T(8,128)(2,1)S(1)} all-gather(bf16[128,1,2,96]{0,3,2,1:T(8,128)(2,1)S(1)} %fusion.22), channel_id=1, replica_groups=mesh['row'=8,'col'=8,'smp'=8] {'row'}, dimensions={0}, use_global_device_ids=true | all-gather | bytes 442368 | tf_op jit(solution)/shard_map/all_gather | solution.py:194
  121.0 1.9 slice_convert_fusion
  122.9 1.3 copy.42
  124.2 1.7 fusion.150
  126.6 1.8 fusion.14
  129.8 1.4 copy.44
  131.2 85.6 %all-reduce.5.cloned.1.call-done = bf16[1,128,768]{2,1,0:T(8,128)(2,1)} async-done(((bf16[1,128,768]{2,1,0:T(8,128)(2,1)}), bf16[1,128,768]{2,1,0:T(8,128)(2,1)}) %all-reduce.5.cloned.1.call-update) | async-done | bytes 196624 | tf_op jit(solution)/shard_map/psum | solution.py:207
  220.7 21.4 %all_gather.21 = bf16[1024,1,2,96]{0,3,2,1:T(8,128)(2,1)S(1)} all-gather(bf16[128,1,2,96]{0,3,2,1:T(8,128)(2,1)S(1)} %fusion.23), channel_id=1, replica_groups=mesh['row'=8,'col'=8,'smp'=8] {'row'}, dimensions={0}, use_global_device_ids=true | all-gather | bytes 442368 | tf_op jit(solution)/shard_map/all_gather | solution.py:194
  243.4 1.8 fusion.15
  246.7 1.3 copy.46
  248.0 77.0 %all-reduce.7.cloned.1.call-done = bf16[1,128,768]{2,1,0:T(8,128)(2,1)} async-done(((bf16[1,128,768]{2,1,0:T(8,128)(2,1)}), bf16[1,128,768]{2,1,0:T(8,128)(2,1)}) %all-reduce.7.cloned.1.call-update) | async-done | bytes 196624 | tf_op jit(solution)/shard_map/psum | solution.py:207
  328.9 21.5 %all_gather.22 = bf16[1024,1,2,96]{0,3,2,1:T(8,128)(2,1)S(1)} all-gather(bf16[128,1,2,96]{0,3,2,1:T(8,128)(2,1)S(1)} %fusion.24), channel_id=1, replica_groups=mesh['row'=8,'col'=8,'smp'=8] {'row'}, dimensions={0}, use_global_device_ids=true | all-gather | bytes 442368 | tf_op jit(solution)/shard_map/all_gather | solution.py:194
  353.3 79.0 %all-reduce.9.cloned.1.call-done = bf16[1,128,768]{2,1,0:T(8,128)(2,1)} async-done(((bf16[1,128,768]{2,1,0:T(8,128)(2,1)}), bf16[1,128,768]{2,1,0:T(8,128)(2,1)}) %all-reduce.9.cloned.1.call-update) | async-done | bytes 196624 | tf_op jit(solution)/shard_map/psum | solution.py:207
  436.1 21.4 %all_gather.23 = bf16[1024,1,2,96]{0,3,2,1:T(8,128)(2,1)S(1)} all-gather(bf16[128,1,2,96]{0,3,2,1:T(8,128)(2,1)S(1)} %fusion.25), channel_id=1, replica_groups=mesh['row'=8,'col'=8,'smp'=8] {'row'}, dimensions={0}, use_global_device_ids=true | all-gather | bytes 442368 | tf_op jit(solution)/shard_map/all_gather | solution.py:194
  459.8 79.7 %all-reduce.11.cloned.1.call-done = bf16[1,128,768]{2,1,0:T(8,128)(2,1)} async-done(((bf16[1,128,768]{2,1,0:T(8,128)(2,1)}), bf16[1,128,768]{2,1,0:T(8,128)(2,1)}) %all-reduce.11.cloned.1.call-update) | async-done | bytes 196624 | tf_op jit(solution)/shard_map/psum | solution.py:207
  (126 shorter events, 29.0 us)
Async XLA Ops:
  7.2 4.8 copy-start
  14.3 17.0 %copy-start.8 = (f32[1,3]{1,0:T(1,128)S(1)}, f32[1,3]{1,0:T(1,128)}, u32[]{:S(2)}) copy-start(f32[1,3]{1,0:T(1,128)} %param.21) | copy-start | bytes 40
  14.3 17.6 %copy-start.14 = (s32[128]{0:T(128)S(1)}, s32[128]{0:T(128)}, u32[]{:S(2)}) copy-start(s32[128]{0:T(128)} %param.18) | copy-start | bytes 1540
  14.3 22.5 %copy-start.6 = (f32[3,8192]{1,0:T(4,128)S(1)}, f32[3,8192]{1,0:T(4,128)}, u32[]{:S(2)}) copy-start(f32[3,8192]{1,0:T(4,128)} %param.17) | copy-start | bytes 294916
  14.3 106.3 %all-to-all-start = ((bf16[4,128,128,1,16]{2,4,3,0,1:T(8,128)(2,1)}), bf16[4,128,128,1,16]{2,4,3,0,1:T(8,128)(2,1)S(1)}, u32[]{:S(2)}, u32[]{:S(2)}) async-start(bf16[4,128,128,1,16]{2,4,3,0,1:T(8,128)(2,1)} %bitcast.262), calls=%async_computation | async-start | bytes 4194304 | tf_op jit(solution)/shard_map/all_to_all | solution.py:74
  31.3 11.5 %copy-start.7 = (f32[4,768]{1,0:T(4,128)S(1)}, f32[4,768]{1,0:T(4,128)}, u32[]{:S(2)}) copy-start(f32[4,768]{1,0:T(4,128)} %param.24) | copy-start | bytes 36868
  31.3 185.6 %all-reduce.5.cloned.1.call-start = ((), (), s32[]{:S(2)}) async-start(), calls=%async_computation.1 | async-start | bytes 393216 | tf_op jit(solution)/shard_map/psum | solution.py:207
  36.8 6.2 %copy-start.11 = (f32[1,3,128]{2,0,1:T(1,128)S(1)}, f32[1,3,128]{2,0,1:T(1,128)}, u32[]{:S(2)}) copy-start(f32[1,3,128]{2,0,1:T(1,128)} %param.23) | copy-start | bytes 4612
  36.9 6.3 %copy-start.5 = (bf16[128,768]{1,0:T(8,128)(2,1)S(1)}, bf16[128,768]{1,0:T(8,128)(2,1)}, u32[]{:S(2)}) copy-start(bf16[128,768]{1,0:T(8,128)(2,1)} %param.15) | copy-start | bytes 589828
  36.9 8.1 %copy-start.9 = (s32[128]{0:T(128)S(1)}, s32[128]{0:T(128)}, u32[]{:S(2)}) copy-start(s32[128]{0:T(128)} %param.19) | copy-start | bytes 1540
  36.9 49.2 %copy-start.12 = (s32[128]{0:T(128)S(1)}, s32[128]{0:T(128)}, u32[]{:S(2)}) copy-start(s32[128]{0:T(128)} %param.20) | copy-start | bytes 1540
  36.9 60.7 %copy-start.10 = (f32[4,16]{1,0:T(4,128)S(1)}, f32[4,16]{1,0:T(4,128)}, u32[]{:S(2)}) copy-start(f32[4,16]{1,0:T(4,128)} %param.26) | copy-start | bytes 772
  128.5 196.6 %all-reduce.7.cloned.1.call-start = ((), (), s32[]{:S(2)}) async-start(), calls=%async_computation.2 | async-start | bytes 393216 | tf_op jit(solution)/shard_map/psum | solution.py:207
  131.2 111.0 %copy-start.1 = (f32[2,128,1024]{2,1,0:T(8,128)S(1)}, f32[2,128,1024]{2,1,0:T(8,128)}, u32[]{:S(2)}) copy-start(f32[2,128,1024]{2,1,0:T(8,128)} %copy.44) | copy-start | bytes 3145732
  245.3 187.0 %all-reduce.9.cloned.1.call-start = ((), (), s32[]{:S(2)}) async-start(), calls=%async_computation.3 | async-start | bytes 393216 | tf_op jit(solution)/shard_map/psum | solution.py:207
  248.0 102.4 %copy-start.2 = (f32[2,128,1024]{2,1,0:T(8,128)S(1)}, f32[2,128,1024]{2,1,0:T(8,128)}, u32[]{:S(2)}) copy-start(f32[2,128,1024]{2,1,0:T(8,128)} %copy.46) | copy-start | bytes 3145732
  350.4 1.2 copy-start.4
  352.6 186.8 %all-reduce.11.cloned.1.call-start = ((), (), s32[]{:S(2)}) async-start(), calls=%async_computation.4 | async-start | bytes 393216 | tf_op jit(solution)/shard_map/psum | solution.py:207
  458.1 82.6 %copy-start.13 = (bf16[3,768]{1,0:T(4,128)(2,1)S(1)}, bf16[3,768]{1,0:T(4,128)(2,1)}, u32[]{:S(2)}) copy-start(bf16[3,768]{1,0:T(4,128)(2,1)} %param.29) | copy-start | bytes 13828
  540.5 1.1 copy-start.3
Sparse Core Ops, SparseCore 0:
  128.6 88.2 all-reduce.4
  245.4 79.6 all-reduce.6
  352.7 79.4 all-reduce.8
  459.8 79.5 all-reduce.10
where the time goes:
time: 549 us; the launch traced here: 548 us
  waiting for transfers between devices  321 us (58%)
  blocking collectives  138 us (25%)
  matrix products  20.9 us (4%)
  between operations  19.3 us (4%)
  starting transfers between devices  17.3 us (3%)
  local copies, waits for them, and re-layouts  16.9 us (3%)
  other arithmetic  14 us (3%)
    psum x4, waiting for transfers between devices, body(): lax.psum(partial_out.astype(jnp.bfloat16), 'col').astype(jnp.float32)  321 us
    all_gather x4, blocking collectives, body(): lax.all_gather(key_value, 'row', axis=0, tiled=True)  85.7 us
    all_gather x1, blocking collectives, body(): lax.all_gather(chain_label, 'row', axis=0, tiled=True)  41.1 us
    all_to_all x1, starting transfers between devices, relay_bias(): lax.all_to_all(spread, ('col', 'smp'), split_axis=1, concat_axis=3, tiled...  16.9 us
    all_gather x1, blocking collectives, body(): lax.all_gather(padding_key_mask, 'row', axis=0, tiled=True)  11.5 us
  transfers between devices with their start and end apart: 5, of which 4 were waited for; matrix products, arithmetic and copies ran while one was open for 3% of the time, Pallas kernels for 0%

commit v1 on v0

--- a/solution.py
+++ b/solution.py
@@ -6,6 +6,7 @@
 EPSILON = 1e-05
 MASKED = -1000000000.0
 LOWEST = -1e30
+push_indices_here = lambda array_in, mesh_name: jnp.sum(lax.all_gather(array_in, mesh_name), 0)
 
 
 def layer_norm(inputs):
@@ -204,7 +205,7 @@
             attention_output_weight[block_index],
             preferred_element_type=jnp.float32,
         )
-        summed = lax.psum(partial_out.astype(jnp.bfloat16), "col").astype(jnp.float32)
+        summed = push_indices_here(partial_out.astype(jnp.bfloat16), "col").astype(jnp.float32)
         hidden_activity = (hidden_activity.astype(jnp.float32) + summed).astype(jnp.bfloat16)
     final_normed = layer_norm(hidden_activity.astype(jnp.float32)).astype(jnp.bfloat16)
     update = jnp.einsum(

time: 549 us -> 385 us (0.70)
  the two profiles are of different devices: /device:TPU:17 before, /device:TPU:1 now
where the time goes in v1:
time: 385 us; the launch traced here: 384 us
  waiting for transfers between devices  153 us (40%)
  blocking collectives  139 us (36%)
  matrix products  21 us (5%)
  between operations  19.3 us (5%)
  starting transfers between devices  17.9 us (5%)
  other arithmetic  17 us (4%)
  local copies, waits for them, and re-layouts  16.8 us (4%)
    all_gather x4, waiting for transfers between devices, lax.all_gather(array_in, mesh_name)  153 us
    all_gather x4, blocking collectives, body(): lax.all_gather(key_value, 'row', axis=0, tiled=True)  85.9 us
    all_gather x1, blocking collectives, body(): lax.all_gather(chain_label, 'row', axis=0, tiled=True)  41.7 us
    all_to_all x1, starting transfers between devices, relay_bias(): lax.all_to_all(spread, ('col', 'smp'), split_axis=1, concat_axis=3, tiled...  17.8 us
    all_gather x1, blocking collectives, body(): lax.all_gather(padding_key_mask, 'row', axis=0, tiled=True)  11.5 us
  transfers between devices with their start and end apart: 5, of which 4 were waited for; matrix products, arithmetic and copies ran while one was open for 4% of the time, Pallas kernels for 0%

profile of v1, /device:TPU:1, one launch (start us, length us, event | category | flops | bytes accessed | tf_op | source)
XLA Modules:
  0.0 384.2 jit_solution(1937159168932150434)
XLA Ops:
  8.6 1.7 fusion.32
  10.3 1.6 fusion.46
  12.4 1.9 broadcast_in_dim.47
  14.3 17.8 %all-to-all-start = ((bf16[4,128,128,1,16]{2,4,3,0,1:T(8,128)(2,1)}), bf16[4,128,128,1,16]{2,4,3,0,1:T(8,128)(2,1)S(1)}, u32[]{:S(2)}, u32[]{:S(2)}) async-start(bf16[4,128,128,1,16]{2,4,3,0,1:T(8,128)(2,1)} %bitcast.246), calls=%async_computation | async-start | bytes 4194304 | tf_op jit(solution)/shard_map/all_to_all | solution.py:75
  37.7 2.6 copy.35
  40.4 2.8 gather_fusion
  45.8 41.7 %all-gather.5 = s32[8,1,128]{2,1,0:T(1,128)S(1)} all-gather(s32[1,1,128]{2,1,0:T(1,128)S(1)} %bitcast.279), channel_id=1, replica_groups=mesh['row'=8,'col'=8,'smp'=8] {'row'}, dimensions={0}, use_global_device_ids=true | all-gather | bytes 4608 | tf_op jit(solution)/shard_map/all_gather | solution.py:152
  87.6 11.5 %all-gather.4 = s32[8,1,128]{2,1,0:T(1,128)S(1)} all-gather(s32[1,1,128]{2,1,0:T(1,128)S(1)} %bitcast.280), channel_id=1, replica_groups=mesh['row'=8,'col'=8,'smp'=8] {'row'}, dimensions={0}, use_global_device_ids=true | all-gather | bytes 4608 | tf_op jit(solution)/shard_map/all_gather | solution.py:153
  100.4 21.4 %all_gather.43 = bf16[1024,1,2,96]{0,3,2,1:T(8,128)(2,1)S(1)} all-gather(bf16[128,1,2,96]{0,3,2,1:T(8,128)(2,1)S(1)} %fusion.18), channel_id=1, replica_groups=mesh['row'=8,'col'=8,'smp'=8] {'row'}, dimensions={0}, use_global_device_ids=true | all-gather | bytes 442368 | tf_op jit(solution)/shard_map/all_gather | solution.py:195
  122.3 1.8 slice_convert_fusion
  125.5 1.7 fusion.144
  128.0 1.8 convolution_convert_fusion.4
  132.5 42.8 %all-gather.11.cloned.1.call-done = bf16[1024,768]{1,0:T(8,128)(2,1)} async-done(((bf16[128,768]{1,0:T(8,128)(2,1)}), bf16[1024,768]{1,0:T(8,128)(2,1)}) %all-gather.11.cloned.1.call-update) | async-done | bytes 1572880 | tf_op jit(solution)/shard_map/all_gather | solution.py:9
  175.3 1.7 reduce.44
  180.0 21.4 %all_gather.47 = bf16[1024,1,2,96]{0,3,2,1:T(8,128)(2,1)S(1)} all-gather(bf16[128,1,2,96]{0,3,2,1:T(8,128)(2,1)S(1)} %fusion.19), channel_id=1, replica_groups=mesh['row'=8,'col'=8,'smp'=8] {'row'}, dimensions={0}, use_global_device_ids=true | all-gather | bytes 442368 | tf_op jit(solution)/shard_map/all_gather | solution.py:195
  202.7 1.8 convolution_convert_fusion.3
  207.3 35.1 %all-gather.13.cloned.1.call-done = bf16[1024,768]{1,0:T(8,128)(2,1)} async-done(((bf16[128,768]{1,0:T(8,128)(2,1)}), bf16[1024,768]{1,0:T(8,128)(2,1)}) %all-gather.13.cloned.1.call-update) | async-done | bytes 1572880 | tf_op jit(solution)/shard_map/all_gather | solution.py:9
  242.4 1.7 reduce.45
  247.1 21.6 %all_gather.50 = bf16[1024,1,2,96]{0,3,2,1:T(8,128)(2,1)S(1)} all-gather(bf16[128,1,2,96]{0,3,2,1:T(8,128)(2,1)S(1)} %fusion.20), channel_id=1, replica_groups=mesh['row'=8,'col'=8,'smp'=8] {'row'}, dimensions={0}, use_global_device_ids=true | all-gather | bytes 442368 | tf_op jit(solution)/shard_map/all_gather | solution.py:195
  271.4 37.4 %all-gather.15.cloned.1.call-done = bf16[1024,768]{1,0:T(8,128)(2,1)} async-done(((bf16[128,768]{1,0:T(8,128)(2,1)}), bf16[1024,768]{1,0:T(8,128)(2,1)}) %all-gather.15.cloned.1.call-update) | async-done | bytes 1572880 | tf_op jit(solution)/shard_map/all_gather | solution.py:9
  308.8 1.6 reduce.46
  313.4 21.5 %all_gather.53 = bf16[1024,1,2,96]{0,3,2,1:T(8,128)(2,1)S(1)} all-gather(bf16[128,1,2,96]{0,3,2,1:T(8,128)(2,1)S(1)} %fusion.21), channel_id=1, replica_groups=mesh['row'=8,'col'=8,'smp'=8] {'row'}, dimensions={0}, use_global_device_ids=true | all-gather | bytes 442368 | tf_op jit(solution)/shard_map/all_gather | solution.py:195
  337.1 37.8 %all-gather.17.cloned.1.call-done = bf16[1024,768]{1,0:T(8,128)(2,1)} async-done(((bf16[128,768]{1,0:T(8,128)(2,1)}), bf16[1024,768]{1,0:T(8,128)(2,1)}) %all-gather.17.cloned.1.call-update) | async-done | bytes 1572880 | tf_op jit(solution)/shard_map/all_gather | solution.py:9
  374.9 1.6 reduce.47
  (130 shorter events, 30.5 us)
Async XLA Ops:
  7.2 4.8 %copy-start = (bf16[128,4,16]{0,2,1:T(8,128)(2,1)S(1)}, bf16[128,4,16]{0,2,1:T(8,128)(2,1)}, u32[]{:S(2)}) copy-start(bf16[128,4,16]{0,2,1:T(8,128)(2,1)} %param.25) | copy-start | bytes 49156
  14.3 17.8 %copy-start.8 = (f32[1,3]{1,0:T(1,128)S(1)}, f32[1,3]{1,0:T(1,128)}, u32[]{:S(2)}) copy-start(f32[1,3]{1,0:T(1,128)} %param.21) | copy-start | bytes 40
  14.3 18.4 %copy-start.14 = (s32[128]{0:T(128)S(1)}, s32[128]{0:T(128)}, u32[]{:S(2)}) copy-start(s32[128]{0:T(128)} %param.18) | copy-start | bytes 1540
  14.3 23.4 %copy-start.6 = (f32[3,8192]{1,0:T(4,128)S(1)}, f32[3,8192]{1,0:T(4,128)}, u32[]{:S(2)}) copy-start(f32[3,8192]{1,0:T(4,128)} %param.17) | copy-start | bytes 294916
  14.3 107.6 %all-to-all-start = ((bf16[4,128,128,1,16]{2,4,3,0,1:T(8,128)(2,1)}), bf16[4,128,128,1,16]{2,4,3,0,1:T(8,128)(2,1)S(1)}, u32[]{:S(2)}, u32[]{:S(2)}) async-start(bf16[4,128,128,1,16]{2,4,3,0,1:T(8,128)(2,1)} %bitcast.246), calls=%async_computation | async-start | bytes 4194304 | tf_op jit(solution)/shard_map/all_to_all | solution.py:75
  32.1 11.5 %copy-start.7 = (f32[4,768]{1,0:T(4,128)S(1)}, f32[4,768]{1,0:T(4,128)}, u32[]{:S(2)}) copy-start(f32[4,768]{1,0:T(4,128)} %param.24) | copy-start | bytes 36868
  32.1 143.2 %all-gather.11.cloned.1.call-start = ((), (), s32[]{:S(2)}) async-start(), calls=%async_computation.1 | async-start | bytes 1769472 | tf_op jit(solution)/shard_map/all_gather | solution.py:9
  37.7 6.2 %copy-start.11 = (f32[1,3,128]{2,0,1:T(1,128)S(1)}, f32[1,3,128]{2,0,1:T(1,128)}, u32[]{:S(2)}) copy-start(f32[1,3,128]{2,0,1:T(1,128)} %param.23) | copy-start | bytes 4612
  37.7 6.3 %copy-start.5 = (bf16[128,768]{1,0:T(8,128)(2,1)S(1)}, bf16[128,768]{1,0:T(8,128)(2,1)}, u32[]{:S(2)}) copy-start(bf16[128,768]{1,0:T(8,128)(2,1)} %param.15) | copy-start | bytes 589828
  37.7 8.1 %copy-start.9 = (s32[128]{0:T(128)S(1)}, s32[128]{0:T(128)}, u32[]{:S(2)}) copy-start(s32[128]{0:T(128)} %param.19) | copy-start | bytes 1540
  37.7 49.8 %copy-start.12 = (s32[128]{0:T(128)S(1)}, s32[128]{0:T(128)}, u32[]{:S(2)}) copy-start(s32[128]{0:T(128)} %param.20) | copy-start | bytes 1540
  37.7 61.3 %copy-start.10 = (f32[4,16]{1,0:T(4,128)S(1)}, f32[4,16]{1,0:T(4,128)}, u32[]{:S(2)}) copy-start(f32[4,16]{1,0:T(4,128)} %param.26) | copy-start | bytes 772
  129.8 112.6 %all-gather.13.cloned.1.call-start = ((), (), s32[]{:S(2)}) async-start(), calls=%async_computation.2 | async-start | bytes 1769472 | tf_op jit(solution)/shard_map/all_gather | solution.py:9
  175.3 26.2 %copy-start.1 = (f32[2,128,1024]{2,1,0:T(8,128)S(1)}, f32[2,128,1024]{2,1,0:T(8,128)}, u32[]{:S(2)}) copy-start(f32[2,128,1024]{2,1,0:T(8,128)} %copy.44) | copy-start | bytes 3145732
  204.6 104.2 %all-gather.15.cloned.1.call-start = ((), (), s32[]{:S(2)}) async-start(), calls=%async_computation.3 | async-start | bytes 1769472 | tf_op jit(solution)/shard_map/all_gather | solution.py:9
  242.4 26.4 %copy-start.2 = (f32[2,128,1024]{2,1,0:T(8,128)S(1)}, f32[2,128,1024]{2,1,0:T(8,128)}, u32[]{:S(2)}) copy-start(f32[2,128,1024]{2,1,0:T(8,128)} %copy.46) | copy-start | bytes 3145732
  268.8 1.2 copy-start.4
  271.0 103.9 %all-gather.17.cloned.1.call-start = ((), (), s32[]{:S(2)}) async-start(), calls=%async_computation.4 | async-start | bytes 1769472 | tf_op jit(solution)/shard_map/all_gather | solution.py:9
  335.7 41.2 %copy-start.13 = (bf16[3,768]{1,0:T(4,128)(2,1)S(1)}, bf16[3,768]{1,0:T(4,128)(2,1)}, u32[]{:S(2)}) copy-start(bf16[3,768]{1,0:T(4,128)(2,1)} %param.29) | copy-start | bytes 13828
  376.6 1.1 copy-start.3
Sparse Core Ops, SparseCore 0:
  129.9 45.3 all-gather.10
  204.7 37.6 all-gather.12
  271.1 37.6 all-gather.14
  337.2 37.6 all-gather.16
